TPU v7x, 512 devices: a whole 4x4x16 slice. The times are simulated.
512 devices in a mesh: replica: 64 (over z, x), shard: 8 (over y, core).
Axes of the slice: x: 4, y: 4, z: 16, core: 2. Of those that a mesh axis runs over, the one named last changes fastest.
Arguments:
- grad_query: float32 [512, 512, 384], P(('replica', 'shard')), may hold values from -1.25 to 1.25
- grad_output: float32 [512, 384, 512], P(('replica', 'shard')), may hold values from -1.25 to 1.25
- grad_norm: float32 [512, 512], P(('replica', 'shard')), may hold values from -1.25 to 1.25
- grad_bias: float32 [512, 32, 6], P(('replica', 'shard')), may hold values from -0.3 to 0.3
- weight_query: float32 [512, 384], P('shard'), may hold values from -5.303301 to 5.303301
- weight_output: float32 [384, 512], P('shard'), may hold values from -6.1237244 to 6.1237244
- weight_norm: float32 [512], P('shard'), may hold values from 0 to 120
- weight_bias: float32 [32, 6], P('shard'), may hold values from -120 to 120
- first_query: float32 [512, 384], P('shard'), may hold values from -120 to 120
- first_output: float32 [384, 512], P('shard'), may hold values from -120 to 120
- first_norm: float32 [512], P('shard'), may hold values from -120 to 120
- first_bias: float32 [32, 6], P('shard'), may hold values from -120 to 120
- second_query: float32 [512, 384], P('shard'), may hold values from 0.05 to 2
- second_output: float32 [384, 512], P('shard'), may hold values from 0.05 to 2
- second_norm: float32 [512], P('shard'), may hold values from 0.05 to 2
- second_bias: float32 [32, 6], P('shard'), may hold values from 0.05 to 2
Outputs:
- updated_query: bfloat16 [512, 384], replicated
- updated_output: bfloat16 [384, 512], replicated
- updated_norm: bfloat16 [512], replicated
- updated_bias: bfloat16 [32, 6], replicated
- first_query_next: float32 [512, 384], P('shard')
- first_output_next: float32 [384, 512], P('shard')
- first_norm_next: float32 [512], P('shard')
- first_bias_next: float32 [32, 6], P('shard')
- second_query_next: float32 [512, 384], P('shard')
- second_output_next: float32 [384, 512], P('shard')
- second_norm_next: float32 [512], P('shard')
- second_bias_next: float32 [32, 6], P('shard')
- norm_table: float32 [2, 4], replicated
- trust_ratios: float32 [4], replicated
All inputs are finite; a program needn't handle non-finite values.
Results may differ from a plain program's by a relative error of at most 0.008.
Values may be sent and summed in bfloat16 or wider, within the bound.
No kernel may reach another device: no remote copies, remote signals or barrier semaphores. Data moves between devices by JAX's collectives and lax.ppermute only.
A program may use at most 64 MiB of HBM per device.

v0:
```python
import jax
import jax.numpy as jnp
from jax import lax
from jax.sharding import PartitionSpec as P

LANES = 128
SHARD_BITS = (0, 1, 2)
REPLICA_BITS = (3, 5, 4, 6, 7, 8)
AXES = ("replica", "shard")


def step_math(summed, moment, second, weight, decay_rate):
    moment_next = 0.5 * moment + 0.5 * summed
    second_next = 0.5 * second + 0.5 * summed * summed
    update = moment_next / (jnp.sqrt(second_next) + 1e-06) + decay_rate * weight
    return (moment_next, second_next, update)


def padded_width(width, multiple):
    return -(-width // multiple) * multiple


def bit_of(index, bit):
    return index >> bit & 1


def exchange(value, bit, devices):
    return lax.ppermute(value, AXES, [(d, d ^ 1 << bit) for d in range(devices)])


def halve(rows, bits, devices):
    index = lax.axis_index(AXES)
    for bit in bits:
        half = rows.shape[0] // 2
        mine = bit_of(index, bit)
        keep = lax.dynamic_slice_in_dim(rows, mine * half, half, 0)
        send = lax.dynamic_slice_in_dim(rows, (1 - mine) * half, half, 0)
        rows = keep + exchange(send, bit, devices)
    return rows


def double(rows, bits, devices):
    index = lax.axis_index(AXES)
    for bit in reversed(bits):
        other = exchange(rows, bit, devices)
        first = bit_of(index, bit) == 0
        rows = jnp.concatenate(
            [jnp.where(first, rows, other), jnp.where(first, other, rows)], axis=0
        )
    return rows


def on_device(
    grad_query,
    grad_output,
    grad_norm,
    grad_bias,
    weight_query,
    weight_output,
    weight_norm,
    weight_bias,
    first_query,
    first_output,
    first_norm,
    first_bias,
    second_query,
    second_output,
    second_norm,
    second_bias,
    shards,
    replicas,
):
    weights = (weight_query, weight_output, weight_norm, weight_bias)
    moments = (first_query, first_output, first_norm, first_bias)
    seconds = (second_query, second_output, second_norm, second_bias)
    decay_rates = (0.01, 0.01, 0.0, 0.0)
    gradients = (grad_query[0], grad_output[0], grad_norm[0], grad_bias[0])
    sizes = [weight.size for weight in weights]
    offsets = [sum(sizes[:member]) for member in range(4)]
    total = sum(sizes)
    devices = shards * replicas
    width = padded_width(total, LANES * replicas)
    levels = len(SHARD_BITS)
    position = [
        sum(((s >> SHARD_BITS[j] & 1) << levels - 1 - j for j in range(levels)))
        for s in range(shards)
    ]
    blocks = [gradient.reshape(shards, -1) for gradient in gradients]
    filler = jnp.zeros((width - total,), jnp.float32)
    packed = jnp.stack(
        [
            jnp.concatenate([block[position.index(p)] for block in blocks] + [filler])
            for p in range(shards)
        ]
    )
    chunks = packed.reshape(shards * replicas * (width // replicas // LANES), LANES)
    mine = halve(chunks, SHARD_BITS + REPLICA_BITS, devices)
    block = double(mine, REPLICA_BITS, devices)
    summed_flat = block.reshape(width)
    summed_all = [
        summed_flat[offsets[member] : offsets[member] + sizes[member]].reshape(
            weights[member].shape
        )
        for member in range(4)
    ]
    results = [
        step_math(
            summed_all[member],
            moments[member],
            seconds[member],
            weights[member],
            decay_rates[member],
        )
        for member in range(4)
    ]
    weight_squares = [jnp.sum(weight * weight) for weight in weights]
    update_squares = [jnp.sum(result[2] * result[2]) for result in results]
    squares = lax.psum(jnp.stack(weight_squares + update_squares), "shard")
    weight_sizes = jnp.sqrt(squares[:4])
    update_sizes = jnp.sqrt(squares[4:])
    trust_ratios = weight_sizes / (update_sizes + 1e-06)
    shards_out = [
        (weights[member] - 0.01 * trust_ratios[member] * results[member][2])
        .astype(jnp.bfloat16)
        .reshape(-1)
        for member in range(4)
    ]
    out_width = padded_width(total, LANES)
    shards_out.append(jnp.zeros((out_width - total,), jnp.bfloat16))
    gathered = lax.all_gather(jnp.concatenate(shards_out), "shard", axis=0, tiled=False)
    full = [
        gathered[:, offsets[member] : offsets[member] + sizes[member]].reshape(
            (shards * weights[member].shape[0],) + weights[member].shape[1:]
        )
        for member in range(4)
    ]
    norm_table = jnp.stack([weight_sizes, update_sizes])
    return (
        full[0],
        full[1],
        full[2],
        full[3],
        results[0][0],
        results[1][0],
        results[2][0],
        results[3][0],
        results[0][1],
        results[1][1],
        results[2][1],
        results[3][1],
        norm_table,
        trust_ratios,
    )


def solution(mesh):
    shards = mesh.shape["shard"]
    replicas = mesh.shape["replica"]
    placed = (
        P(("replica", "shard"), None, None),
        P(("replica", "shard"), None, None),
        P(("replica", "shard"), None),
        P(("replica", "shard"), None, None),
        P("shard", None),
        P("shard", None),
        P("shard"),
        P("shard", None),
        P("shard", None),
        P("shard", None),
        P("shard"),
        P("shard", None),
        P("shard", None),
        P("shard", None),
        P("shard"),
        P("shard", None),
    )

    def body(*args):
        return on_device(*args, shards=shards, replicas=replicas)

    return jax.shard_map(
        body,
        mesh=mesh,
        in_specs=placed,
        out_specs=(
            P(),
            P(),
            P(),
            P(),
            P("shard", None),
            P("shard", None),
            P("shard"),
            P("shard", None),
            P("shard", None),
            P("shard", None),
            P("shard"),
            P("shard", None),
            P(),
            P(),
        ),
        check_vma=False,
    )
```

profile of v0, /device:TPU:1, one launch (start us, length us, event | category | flops | bytes accessed | tf_op | source)
XLA Modules:
  0.0 204.9 jit_solution(14163425917352322013)
XLA Ops:
  11.2 3.6 %concatenate.47 = f32[57344]{0:T(1024)} concatenate(f32[24576]{0:T(1024)S(1)} %squeeze.108, f32[24576]{0:T(1024)S(1)} %bitcast.90, f32[64]{0:T(128)S(1)} %get-tuple-element.117, f32[24]{0:T(128)S(1)} %squeeze.111, f32[8104]{0:T(1024)S(1)} %broadcast_in_dim.6), dimensions={0} | concatenate | bytes 458752 | tf_op jit(solution)/shard_map/concatenate | solution.py:92
  14.8 4.5 %stack.75 = f32[8,57344]{1,0:T(8,128)S(1)} concatenate(f32[1,57344]{1,0:T(1,128)S(1)} %bitcast.80, f32[1,57344]{1,0:T(1,128)S(1)} %bitcast.81, f32[1,57344]{1,0:T(1,128)} %bitcast.82, f32[1,57344]{1,0:T(1,128)S(1)} %bitcast.75, f32[1,57344]{1,0:T(1,128)S(1)} %bitcast.76, f32[1,57344]{1,0:T(1,128)S(1)} %bitcast.77, f32[1,57344]{1,0:T(1,128)S(1)} %bitcast.78, f32[1,57344]{1,0:T(1,128)S(1)} %bitcast.79), dimensions={0} | concatenate | bytes 3670016 | tf_op jit(solution)/shard_map/stack | solution.py:90
  22.3 8.8 %collective-permute-start = (f32[1792,128]{1,0:T(8,128)S(1)}, f32[1792,128]{1,0:T(8,128)}, u32[]{:S(2)}, u32[]{:S(2)}) collective-permute-start(f32[1792,128]{1,0:T(8,128)S(1)} %constant_dynamic-slice_fusion.9), channel_id=1, source_target_pairs={{0,1},{1,0},{2,3},{3,2},{4,5},{5,4},{6,7},{7,6},{8,9},{9,8},{10,11... | collective-permute-start | bytes 2752520 | tf_op jit(solution)/shard_map/ppermute | solution.py:28
  31.1 2.2 %collective-permute-done = f32[1792,128]{1,0:T(8,128)} collective-permute-done((f32[1792,128]{1,0:T(8,128)S(1)}, f32[1792,128]{1,0:T(8,128)}, u32[]{:S(2)}, u32[]{:S(2)}) %collective-permute-start) | collective-permute-done | bytes 917536 | tf_op jit(solution)/shard_map/ppermute | solution.py:28
  34.6 1.9 collective-permute-start.1
  36.5 11.7 %collective-permute-done.1 = f32[896,128]{1,0:T(8,128)S(1)} collective-permute-done((f32[896,128]{1,0:T(8,128)S(1)}, f32[896,128]{1,0:T(8,128)S(1)}, u32[]{:S(2)}, u32[]{:S(2)}) %collective-permute-start.1) | collective-permute-done | bytes 458784 | tf_op jit(solution)/shard_map/ppermute | solution.py:28
  48.3 1.9 collective-permute-start.2
  50.3 7.4 %collective-permute-done.2 = f32[448,128]{1,0:T(8,128)S(1)} collective-permute-done((f32[448,128]{1,0:T(8,128)S(1)}, f32[448,128]{1,0:T(8,128)S(1)}, u32[]{:S(2)}, u32[]{:S(2)}) %collective-permute-start.2) | collective-permute-done | bytes 229408 | tf_op jit(solution)/shard_map/ppermute | solution.py:28
  59.7 3.5 %collective-permute-done.3 = f32[224,128]{1,0:T(8,128)S(1)} collective-permute-done((f32[224,128]{1,0:T(8,128)S(1)}, f32[224,128]{1,0:T(8,128)S(1)}, u32[]{:S(2)}, u32[]{:S(2)}) %collective-permute-start.3) | collective-permute-done | bytes 114720 | tf_op jit(solution)/shard_map/ppermute | solution.py:28
  65.2 3.0 %collective-permute-done.4 = f32[112,128]{1,0:T(8,128)S(1)} collective-permute-done((f32[112,128]{1,0:T(8,128)S(1)}, f32[112,128]{1,0:T(8,128)S(1)}, u32[]{:S(2)}, u32[]{:S(2)}) %collective-permute-start.4) | collective-permute-done | bytes 57376 | tf_op jit(solution)/shard_map/ppermute | solution.py:28
  70.2 4.1 %collective-permute-done.5 = f32[56,128]{1,0:T(8,128)S(1)} collective-permute-done((f32[56,128]{1,0:T(8,128)S(1)}, f32[56,128]{1,0:T(8,128)S(1)}, u32[]{:S(2)}, u32[]{:S(2)}) %collective-permute-start.5) | collective-permute-done | bytes 28704 | tf_op jit(solution)/shard_map/ppermute | solution.py:28
  74.3 1.9 collective-permute-start.6
  76.3 3.4 %collective-permute-done.6 = f32[28,128]{1,0:T(8,128)S(1)} collective-permute-done((f32[28,128]{1,0:T(8,128)S(1)}, f32[28,128]{1,0:T(8,128)S(1)}, u32[]{:S(2)}, u32[]{:S(2)}) %collective-permute-start.6) | collective-permute-done | bytes 14368 | tf_op jit(solution)/shard_map/ppermute | solution.py:28
  79.7 4.3 %collective-permute-start.7 = (f32[14,128]{1,0:T(8,128)S(1)}, f32[14,128]{1,0:T(8,128)S(1)}, u32[]{:S(2)}, u32[]{:S(2)}) collective-permute-start(f32[14,128]{1,0:T(8,128)S(1)} %constant_dynamic-slice_fusion.2), channel_id=1, source_target_pairs={{0,128},{1,129},{2,130},{3,131},{4,132},{5,133},{6,134},{7,135},{8... | collective-permute-start | bytes 21512 | tf_op jit(solution)/shard_map/ppermute | solution.py:28
  84.0 4.0 %collective-permute-done.7 = f32[14,128]{1,0:T(8,128)S(1)} collective-permute-done((f32[14,128]{1,0:T(8,128)S(1)}, f32[14,128]{1,0:T(8,128)S(1)}, u32[]{:S(2)}, u32[]{:S(2)}) %collective-permute-start.7) | collective-permute-done | bytes 7200 | tf_op jit(solution)/shard_map/ppermute | solution.py:28
  88.1 10.1 %collective-permute-start.8 = (f32[7,128]{1,0:T(8,128)S(1)}, f32[7,128]{1,0:T(8,128)S(1)}, u32[]{:S(2)}, u32[]{:S(2)}) collective-permute-start(f32[7,128]{1,0:T(8,128)S(1)} %constant_dynamic-slice_fusion), channel_id=1, source_target_pairs={{0,256},{1,257},{2,258},{3,259},{4,260},{5,261},{6,262},{7,263},{8... | collective-permute-start | bytes 10760 | tf_op jit(solution)/shard_map/ppermute | solution.py:28
  98.2 3.0 %collective-permute-done.8 = f32[7,128]{1,0:T(8,128)S(1)} collective-permute-done((f32[7,128]{1,0:T(8,128)S(1)}, f32[7,128]{1,0:T(8,128)S(1)}, u32[]{:S(2)}, u32[]{:S(2)}) %collective-permute-start.8) | collective-permute-done | bytes 3616 | tf_op jit(solution)/shard_map/ppermute | solution.py:28
  101.1 10.1 %collective-permute-start.9 = (f32[7,128]{1,0:T(8,128)S(1)}, f32[7,128]{1,0:T(8,128)S(1)}, u32[]{:S(2)}, u32[]{:S(2)}) collective-permute-start(f32[7,128]{1,0:T(8,128)S(1)} %fusion.5), channel_id=1, source_target_pairs={{0,256},{1,257},{2,258},{3,259},{4,260},{5,261},{6,262},{7,263},{8... | collective-permute-start | bytes 10760 | tf_op jit(solution)/shard_map/ppermute | solution.py:28
  111.2 3.0 %collective-permute-done.9 = f32[7,128]{1,0:T(8,128)S(1)} collective-permute-done((f32[7,128]{1,0:T(8,128)S(1)}, f32[7,128]{1,0:T(8,128)S(1)}, u32[]{:S(2)}, u32[]{:S(2)}) %collective-permute-start.9) | collective-permute-done | bytes 3616 | tf_op jit(solution)/shard_map/ppermute | solution.py:28
  114.2 4.3 %collective-permute-start.10 = (f32[14,128]{1,0:T(8,128)S(1)}, f32[14,128]{1,0:T(8,128)S(1)}, u32[]{:S(2)}, u32[]{:S(2)}) collective-permute-start(f32[14,128]{1,0:T(8,128)S(1)} %pad_maximum_fusion.5), channel_id=1, source_target_pairs={{0,128},{1,129},{2,130},{3,131},{4,132},{5,133},{6,134},{7,135},{8... | collective-permute-start | bytes 21512 | tf_op jit(solution)/shard_map/ppermute | solution.py:28
  118.5 4.3 %collective-permute-done.10 = f32[14,128]{1,0:T(8,128)S(1)} collective-permute-done((f32[14,128]{1,0:T(8,128)S(1)}, f32[14,128]{1,0:T(8,128)S(1)}, u32[]{:S(2)}, u32[]{:S(2)}) %collective-permute-start.10) | collective-permute-done | bytes 7200 | tf_op jit(solution)/shard_map/ppermute | solution.py:28
  122.8 1.9 collective-permute-start.11
  124.8 3.4 %collective-permute-done.11 = f32[28,128]{1,0:T(8,128)S(1)} collective-permute-done((f32[28,128]{1,0:T(8,128)S(1)}, f32[28,128]{1,0:T(8,128)S(1)}, u32[]{:S(2)}, u32[]{:S(2)}) %collective-permute-start.11) | collective-permute-done | bytes 14368 | tf_op jit(solution)/shard_map/ppermute | solution.py:28
  128.2 2.6 %collective-permute-start.12 = (f32[56,128]{1,0:T(8,128)S(1)}, f32[56,128]{1,0:T(8,128)S(1)}, u32[]{:S(2)}, u32[]{:S(2)}) collective-permute-start(f32[56,128]{1,0:T(8,128)S(1)} %pad_maximum_fusion.3), channel_id=1, source_target_pairs={{0,16},{1,17},{2,18},{3,19},{4,20},{5,21},{6,22},{7,23},{8,24},{9,... | collective-permute-start | bytes 86024 | tf_op jit(solution)/shard_map/ppermute | solution.py:28
  130.9 3.5 %collective-permute-done.12 = f32[56,128]{1,0:T(8,128)S(1)} collective-permute-done((f32[56,128]{1,0:T(8,128)S(1)}, f32[56,128]{1,0:T(8,128)S(1)}, u32[]{:S(2)}, u32[]{:S(2)}) %collective-permute-start.12) | collective-permute-done | bytes 28704 | tf_op jit(solution)/shard_map/ppermute | solution.py:28
  134.4 2.0 collective-permute-start.13
  136.4 3.2 %collective-permute-done.13 = f32[112,128]{1,0:T(8,128)S(1)} collective-permute-done((f32[112,128]{1,0:T(8,128)S(1)}, f32[112,128]{1,0:T(8,128)S(1)}, u32[]{:S(2)}, u32[]{:S(2)}) %collective-permute-start.13) | collective-permute-done | bytes 57376 | tf_op jit(solution)/shard_map/ppermute | solution.py:28
  139.6 1.9 collective-permute-start.14
  141.6 3.9 %collective-permute-done.14 = f32[224,128]{1,0:T(8,128)S(1)} collective-permute-done((f32[224,128]{1,0:T(8,128)S(1)}, f32[224,128]{1,0:T(8,128)S(1)}, u32[]{:S(2)}, u32[]{:S(2)}) %collective-permute-start.14) | collective-permute-done | bytes 114720 | tf_op jit(solution)/shard_map/ppermute | solution.py:28
  149.6 5.3 %stack.80 = f32[8]{0:T(128)S(1)} concatenate(f32[1]{0:T(128)} %bitcast, f32[1]{0:T(128)} %bitcast.1, f32[1]{0:T(128)} %bitcast.2, f32[1]{0:T(128)} %bitcast.3, f32[1]{0:T(128)} %bitcast.20, f32[1]{0:T(128)} %bitcast.21, f32[1]{0:T(128)} %bitcast.23, f32[1]{0:T(128)} %bitcast.24), dimensions={0} | concatenate | bytes 64 | tf_op jit(solution)/shard_map/stack | solution.py:118
  154.9 26.8 %psum.7 = f32[8]{0:T(128)S(1)} all-reduce(f32[8]{0:T(128)S(1)} %stack.80), channel_id=1, replica_groups=mesh['replica'=64,'shard'=8] {'shard'}, use_global_device_ids=true, to_apply=%region_8.9 | all-reduce | flops 8 | bytes 64 | tf_op jit(solution)/shard_map/psum | solution.py:118
  185.6 15.2 %all-gather.1 = bf16[8,1,49280]{2,1,0:T(2,128)(2,1)S(1)} all-gather(bf16[1,1,49280]{2,1,0:T(2,128)(2,1)S(1)} %reshape.153), channel_id=2, replica_groups=mesh['replica'=64,'shard'=8] {'shard'}, dimensions={0}, use_global_device_ids=true | all-gather | bytes 887040 | tf_op jit(solution)/shard_map/all_gather | solution.py:130
  (151 shorter events, 30.0 us)
Async XLA Ops:
  22.3 11.0 %collective-permute-start = (f32[1792,128]{1,0:T(8,128)S(1)}, f32[1792,128]{1,0:T(8,128)}, u32[]{:S(2)}, u32[]{:S(2)}) collective-permute-start(f32[1792,128]{1,0:T(8,128)S(1)} %constant_dynamic-slice_fusion.9), channel_id=1, source_target_pairs={{0,1},{1,0},{2,3},{3,2},{4,5},{5,4},{6,7},{7,6},{8,9},{9,8},{10,11... | collective-permute-start | bytes 2752520 | tf_op jit(solution)/shard_map/ppermute | solution.py:28
  34.6 13.6 %collective-permute-start.1 = (f32[896,128]{1,0:T(8,128)S(1)}, f32[896,128]{1,0:T(8,128)S(1)}, u32[]{:S(2)}, u32[]{:S(2)}) collective-permute-start(f32[896,128]{1,0:T(8,128)S(1)} %constant_dynamic-slice_fusion.8), channel_id=1, source_target_pairs={{0,2},{1,3},{2,0},{3,1},{4,6},{5,7},{6,4},{7,5},{8,10},{9,11},{10,... | collective-permute-start | bytes 1376264 | tf_op jit(solution)/shard_map/ppermute | solution.py:28
  48.3 9.3 %collective-permute-start.2 = (f32[448,128]{1,0:T(8,128)S(1)}, f32[448,128]{1,0:T(8,128)S(1)}, u32[]{:S(2)}, u32[]{:S(2)}) collective-permute-start(f32[448,128]{1,0:T(8,128)S(1)} %constant_dynamic-slice_fusion.7), channel_id=1, source_target_pairs={{0,4},{1,5},{2,6},{3,7},{4,0},{5,1},{6,2},{7,3},{8,12},{9,13},{10,... | collective-permute-start | bytes 688136 | tf_op jit(solution)/shard_map/ppermute | solution.py:28
  57.7 5.5 %collective-permute-start.3 = (f32[224,128]{1,0:T(8,128)S(1)}, f32[224,128]{1,0:T(8,128)S(1)}, u32[]{:S(2)}, u32[]{:S(2)}) collective-permute-start(f32[224,128]{1,0:T(8,128)S(1)} %constant_dynamic-slice_fusion.6), channel_id=1, source_target_pairs={{0,8},{1,9},{2,10},{3,11},{4,12},{5,13},{6,14},{7,15},{8,0},{9,1},... | collective-permute-start | bytes 344072 | tf_op jit(solution)/shard_map/ppermute | solution.py:28
  59.6 86.2 %copy-start.18 = (f32[64]{0:T(128)S(1)}, f32[64]{0:T(128)}, u32[]{:S(2)}) copy-start(f32[64]{0:T(128)} %param.22) | copy-start | bytes 772
  59.6 86.2 %copy-start.19 = (f32[64]{0:T(128)S(1)}, f32[64]{0:T(128)}, u32[]{:S(2)}) copy-start(f32[64]{0:T(128)} %param.30) | copy-start | bytes 772
  59.6 86.2 %copy-start.20 = (f32[64]{0:T(128)S(1)}, f32[64]{0:T(128)}, u32[]{:S(2)}) copy-start(f32[64]{0:T(128)} %param.26) | copy-start | bytes 772
  59.6 87.3 %copy-start.15 = (f32[4,6]{1,0:T(4,128)S(1)}, f32[4,6]{1,0:T(4,128)}, u32[]{:S(2)}) copy-start(f32[4,6]{1,0:T(4,128)} %param.23) | copy-start | bytes 292
  59.7 87.3 %copy-start.16 = (f32[4,6]{1,0:T(4,128)S(1)}, f32[4,6]{1,0:T(4,128)}, u32[]{:S(2)}) copy-start(f32[4,6]{1,0:T(4,128)} %param.31) | copy-start | bytes 292
  59.7 87.3 %copy-start.17 = (f32[4,6]{1,0:T(4,128)S(1)}, f32[4,6]{1,0:T(4,128)}, u32[]{:S(2)}) copy-start(f32[4,6]{1,0:T(4,128)} %param.27) | copy-start | bytes 292
  59.7 88.5 %copy-start.3 = (f32[64,384]{1,0:T(8,128)S(1)}, f32[64,384]{1,0:T(8,128)}, u32[]{:S(2)}) copy-start(f32[64,384]{1,0:T(8,128)} %param.20) | copy-start | bytes 294916
  59.7 88.5 %copy-start.9 = (f32[64,384]{1,0:T(8,128)S(1)}, f32[64,384]{1,0:T(8,128)}, u32[]{:S(2)}) copy-start(f32[64,384]{1,0:T(8,128)} %param.28) | copy-start | bytes 294916
  59.7 88.5 %copy-start.10 = (f32[64,384]{1,0:T(8,128)S(1)}, f32[64,384]{1,0:T(8,128)}, u32[]{:S(2)}) copy-start(f32[64,384]{1,0:T(8,128)} %param.24) | copy-start | bytes 294916
  63.2 4.9 %collective-permute-start.4 = (f32[112,128]{1,0:T(8,128)S(1)}, f32[112,128]{1,0:T(8,128)S(1)}, u32[]{:S(2)}, u32[]{:S(2)}) collective-permute-start(f32[112,128]{1,0:T(8,128)S(1)} %constant_dynamic-slice_fusion.5), channel_id=1, source_target_pairs={{0,32},{1,33},{2,34},{3,35},{4,36},{5,37},{6,38},{7,39},{8,40},{9,... | collective-permute-start | bytes 172040 | tf_op jit(solution)/shard_map/ppermute | solution.py:28
  68.2 6.1 %collective-permute-start.5 = (f32[56,128]{1,0:T(8,128)S(1)}, f32[56,128]{1,0:T(8,128)S(1)}, u32[]{:S(2)}, u32[]{:S(2)}) collective-permute-start(f32[56,128]{1,0:T(8,128)S(1)} %constant_dynamic-slice_fusion.4), channel_id=1, source_target_pairs={{0,16},{1,17},{2,18},{3,19},{4,20},{5,21},{6,22},{7,23},{8,24},{9,... | collective-permute-start | bytes 86024 | tf_op jit(solution)/shard_map/ppermute | solution.py:28
  70.1 78.8 %copy-start.2 = (f32[48,512]{1,0:T(8,128)S(1)}, f32[48,512]{1,0:T(8,128)}, u32[]{:S(2)}) copy-start(f32[48,512]{1,0:T(8,128)} %param.21) | copy-start | bytes 294916
  70.1 78.8 %copy-start.11 = (f32[48,512]{1,0:T(8,128)S(1)}, f32[48,512]{1,0:T(8,128)}, u32[]{:S(2)}) copy-start(f32[48,512]{1,0:T(8,128)} %param.29) | copy-start | bytes 294916
  70.2 78.7 %copy-start.12 = (f32[48,512]{1,0:T(8,128)S(1)}, f32[48,512]{1,0:T(8,128)}, u32[]{:S(2)}) copy-start(f32[48,512]{1,0:T(8,128)} %param.25) | copy-start | bytes 294916
  74.3 5.4 %collective-permute-start.6 = (f32[28,128]{1,0:T(8,128)S(1)}, f32[28,128]{1,0:T(8,128)S(1)}, u32[]{:S(2)}, u32[]{:S(2)}) collective-permute-start(f32[28,128]{1,0:T(8,128)S(1)} %constant_dynamic-slice_fusion.3), channel_id=1, source_target_pairs={{0,64},{1,65},{2,66},{3,67},{4,68},{5,69},{6,70},{7,71},{8,72},{9,... | collective-permute-start | bytes 43016 | tf_op jit(solution)/shard_map/ppermute | solution.py:28
  79.7 8.3 %collective-permute-start.7 = (f32[14,128]{1,0:T(8,128)S(1)}, f32[14,128]{1,0:T(8,128)S(1)}, u32[]{:S(2)}, u32[]{:S(2)}) collective-permute-start(f32[14,128]{1,0:T(8,128)S(1)} %constant_dynamic-slice_fusion.2), channel_id=1, source_target_pairs={{0,128},{1,129},{2,130},{3,131},{4,132},{5,133},{6,134},{7,135},{8... | collective-permute-start | bytes 21512 | tf_op jit(solution)/shard_map/ppermute | solution.py:28
  88.1 13.1 %collective-permute-start.8 = (f32[7,128]{1,0:T(8,128)S(1)}, f32[7,128]{1,0:T(8,128)S(1)}, u32[]{:S(2)}, u32[]{:S(2)}) collective-permute-start(f32[7,128]{1,0:T(8,128)S(1)} %constant_dynamic-slice_fusion), channel_id=1, source_target_pairs={{0,256},{1,257},{2,258},{3,259},{4,260},{5,261},{6,262},{7,263},{8... | collective-permute-start | bytes 10760 | tf_op jit(solution)/shard_map/ppermute | solution.py:28
  101.1 13.1 %collective-permute-start.9 = (f32[7,128]{1,0:T(8,128)S(1)}, f32[7,128]{1,0:T(8,128)S(1)}, u32[]{:S(2)}, u32[]{:S(2)}) collective-permute-start(f32[7,128]{1,0:T(8,128)S(1)} %fusion.5), channel_id=1, source_target_pairs={{0,256},{1,257},{2,258},{3,259},{4,260},{5,261},{6,262},{7,263},{8... | collective-permute-start | bytes 10760 | tf_op jit(solution)/shard_map/ppermute | solution.py:28
  114.2 8.6 %collective-permute-start.10 = (f32[14,128]{1,0:T(8,128)S(1)}, f32[14,128]{1,0:T(8,128)S(1)}, u32[]{:S(2)}, u32[]{:S(2)}) collective-permute-start(f32[14,128]{1,0:T(8,128)S(1)} %pad_maximum_fusion.5), channel_id=1, source_target_pairs={{0,128},{1,129},{2,130},{3,131},{4,132},{5,133},{6,134},{7,135},{8... | collective-permute-start | bytes 21512 | tf_op jit(solution)/shard_map/ppermute | solution.py:28
  122.8 5.4 %collective-permute-start.11 = (f32[28,128]{1,0:T(8,128)S(1)}, f32[28,128]{1,0:T(8,128)S(1)}, u32[]{:S(2)}, u32[]{:S(2)}) collective-permute-start(f32[28,128]{1,0:T(8,128)S(1)} %pad_maximum_fusion.4), channel_id=1, source_target_pairs={{0,64},{1,65},{2,66},{3,67},{4,68},{5,69},{6,70},{7,71},{8,72},{9,... | collective-permute-start | bytes 43016 | tf_op jit(solution)/shard_map/ppermute | solution.py:28
  128.2 6.1 %collective-permute-start.12 = (f32[56,128]{1,0:T(8,128)S(1)}, f32[56,128]{1,0:T(8,128)S(1)}, u32[]{:S(2)}, u32[]{:S(2)}) collective-permute-start(f32[56,128]{1,0:T(8,128)S(1)} %pad_maximum_fusion.3), channel_id=1, source_target_pairs={{0,16},{1,17},{2,18},{3,19},{4,20},{5,21},{6,22},{7,23},{8,24},{9,... | collective-permute-start | bytes 86024 | tf_op jit(solution)/shard_map/ppermute | solution.py:28
  134.4 5.2 %collective-permute-start.13 = (f32[112,128]{1,0:T(8,128)S(1)}, f32[112,128]{1,0:T(8,128)S(1)}, u32[]{:S(2)}, u32[]{:S(2)}) collective-permute-start(f32[112,128]{1,0:T(8,128)S(1)} %pad_maximum_fusion.2), channel_id=1, source_target_pairs={{0,32},{1,33},{2,34},{3,35},{4,36},{5,37},{6,38},{7,39},{8,40},{9,... | collective-permute-start | bytes 172040 | tf_op jit(solution)/shard_map/ppermute | solution.py:28
  139.6 5.8 %collective-permute-start.14 = (f32[224,128]{1,0:T(8,128)S(1)}, f32[224,128]{1,0:T(8,128)S(1)}, u32[]{:S(2)}, u32[]{:S(2)}) collective-permute-start(f32[224,128]{1,0:T(8,128)S(1)} %pad_maximum_fusion.1), channel_id=1, source_target_pairs={{0,8},{1,9},{2,10},{3,11},{4,12},{5,13},{6,14},{7,15},{8,0},{9,1},... | collective-permute-start | bytes 344072 | tf_op jit(solution)/shard_map/ppermute | solution.py:28
  148.9 51.9 %copy-start.4 = (f32[64,384]{1,0:T(8,128)}, f32[64,384]{1,0:T(8,128)S(1)}, u32[]{:S(2)}) copy-start(f32[64,384]{1,0:T(8,128)S(1)} %get-tuple-element.70) | copy-start | bytes 294916
  148.9 51.9 %copy-start.5 = (f32[64,384]{1,0:T(8,128)}, f32[64,384]{1,0:T(8,128)S(1)}, u32[]{:S(2)}) copy-start(f32[64,384]{1,0:T(8,128)S(1)} %get-tuple-element.71) | copy-start | bytes 294916
  149.6 51.3 %copy-start.6 = (f32[48,512]{1,0:T(8,128)}, f32[48,512]{1,0:T(8,128)S(1)}, u32[]{:S(2)}) copy-start(f32[48,512]{1,0:T(8,128)S(1)} %get-tuple-element.68) | copy-start | bytes 294916
  149.6 51.3 %copy-start.7 = (f32[48,512]{1,0:T(8,128)}, f32[48,512]{1,0:T(8,128)S(1)}, u32[]{:S(2)}) copy-start(f32[48,512]{1,0:T(8,128)S(1)} %get-tuple-element.69) | copy-start | bytes 294916
  181.8 19.1 %copy-start.13 = (f32[4]{0:T(128)}, f32[4]{0:T(128)S(1)}, u32[]{:S(2)}) copy-start(f32[4]{0:T(128)S(1)} %get-tuple-element.123) | copy-start | bytes 52
  (4 other events, 17.2 us)
where the time goes:
time: 206 us; the launch traced here: 205 us
  waiting for transfers between devices  63.6 us (31%)
  starting transfers between devices  57.5 us (28%)
  blocking collectives  42 us (20%)
  local copies, waits for them, and re-layouts  31.6 us (15%)
  other arithmetic  6.09 us (3%)
  between operations  4.1 us (2%)
    ppermute x15, waiting for transfers between devices, exchange(): lax.ppermute(value, AXES, [(d, d ^ 1 << bit) for d in range(devices)])  63.6 us
    ppermute x15, starting transfers between devices, exchange(): lax.ppermute(value, AXES, [(d, d ^ 1 << bit) for d in range(devices)])  57.5 us
    psum x1, blocking collectives, on_device(): squares = lax.psum(jnp.stack(weight_squares + update_squares), 'shard')  26.8 us
    all_gather x1, blocking collectives, on_device(): lax.all_gather(jnp.concatenate(shards_out), 'shard', axis=0, tiled=False)  15.2 us
    concatenate x8, local copies, waits for them, and re-layouts, on_device(): jnp.concatenate([block[position.index(p)] for block in blocks] + [filler])  10.6 us
    another operation x1, local copies, waits for them, and re-layouts, on_device(): squares = lax.psum(jnp.stack(weight_squares + update_squares), 'shard')  5.32 us
    another operation x1, local copies, waits for them, and re-layouts, on_device(): jnp.stack([jnp.concatenate([block[position.index(p)] for block in blocks]...  4.55 us
  transfers between devices with their start and end apart: 15, of which 15 were waited for; matrix products, arithmetic and copies ran while one was open for 0% of the time, Pallas kernels for 0%

commit v1 on v0

--- a/solution.py
+++ b/solution.py
@@ -115,7 +115,7 @@
     ]
     weight_squares = [jnp.sum(weight * weight) for weight in weights]
     update_squares = [jnp.sum(result[2] * result[2]) for result in results]
-    squares = lax.psum(jnp.stack(weight_squares + update_squares), "shard")
+    squares = jnp.sum(lax.all_gather(jnp.stack(weight_squares + update_squares), "shard"), axis=0)
     weight_sizes = jnp.sqrt(squares[:4])
     update_sizes = jnp.sqrt(squares[4:])
     trust_ratios = weight_sizes / (update_sizes + 1e-06)

time: 206 us -> 206 us (level)
    psum x1 -> x0, blocking collectives: 26.8 us -> none  [on_device(): squares = lax.psum(jnp.stack(weight_squares + update_squares), 'shard')]
    unnamed x0 -> x1, blocking collectives: none -> 26.8 us
  transfers between devices with their start and end apart: 15 -> 15, of which waited for: 15 -> 15; matrix products, arithmetic and copies ran while one was open for 0% -> 1% of each run, Pallas kernels for 0% -> 0%
where the time goes in v1:
time: 206 us; the launch traced here: 205 us
  waiting for transfers between devices  61.7 us (30%)
  starting transfers between devices  57.6 us (28%)
  blocking collectives  42 us (20%)
  local copies, waits for them, and re-layouts  33.1 us (16%)
  other arithmetic  6.11 us (3%)
  between operations  4.76 us (2%)
    ppermute x15, waiting for transfers between devices, exchange(): lax.ppermute(value, AXES, [(d, d ^ 1 << bit) for d in range(devices)])  61.7 us
    ppermute x15, starting transfers between devices, exchange(): lax.ppermute(value, AXES, [(d, d ^ 1 << bit) for d in range(devices)])  57.6 us
    unnamed x1, blocking collectives  26.8 us
    all_gather x1, blocking collectives, on_device(): lax.all_gather(jnp.concatenate(shards_out), 'shard', axis=0, tiled=False)  15.2 us
    concatenate x8, local copies, waits for them, and re-layouts, on_device(): jnp.concatenate([block[position.index(p)] for block in blocks] + [filler])  10.6 us
    another operation x1, local copies, waits for them, and re-layouts, on_device(): jnp.stack(weight_squares + update_squares)  5.22 us
    another operation x1, local copies, waits for them, and re-layouts, on_device(): jnp.stack([jnp.concatenate([block[position.index(p)] for block in blocks]...  4.55 us
  transfers between devices with their start and end apart: 15, of which 15 were waited for; matrix products, arithmetic and copies ran while one was open for 1% of the time, Pallas kernels for 0%

profile of v1, /device:TPU:1, one launch (start us, length us, event | category | flops | bytes accessed | tf_op | source)
XLA Modules:
  0.0 205.3 jit_solution(4084951005706063503)
XLA Ops:
  11.2 3.6 %concatenate.47 = f32[57344]{0:T(1024)} concatenate(f32[24576]{0:T(1024)S(1)} %squeeze.108, f32[24576]{0:T(1024)S(1)} %bitcast.91, f32[64]{0:T(128)S(1)} %get-tuple-element.117, f32[24]{0:T(128)S(1)} %squeeze.111, f32[8104]{0:T(1024)S(1)} %broadcast_in_dim.6), dimensions={0} | concatenate | bytes 458752 | tf_op jit(solution)/shard_map/concatenate | solution.py:92
  14.8 4.5 %stack.75 = f32[8,57344]{1,0:T(8,128)S(1)} concatenate(f32[1,57344]{1,0:T(1,128)S(1)} %bitcast.81, f32[1,57344]{1,0:T(1,128)S(1)} %bitcast.82, f32[1,57344]{1,0:T(1,128)} %bitcast.83, f32[1,57344]{1,0:T(1,128)S(1)} %bitcast.76, f32[1,57344]{1,0:T(1,128)S(1)} %bitcast.77, f32[1,57344]{1,0:T(1,128)S(1)} %bitcast.78, f32[1,57344]{1,0:T(1,128)S(1)} %bitcast.79, f32[1,57344]{1,0:T(1,128)S(1)} %bitcast.80), dimensions={0} | concatenate | bytes 3670016 | tf_op jit(solution)/shard_map/stack | solution.py:90
  22.3 8.8 %collective-permute-start = (f32[1792,128]{1,0:T(8,128)S(1)}, f32[1792,128]{1,0:T(8,128)}, u32[]{:S(2)}, u32[]{:S(2)}) collective-permute-start(f32[1792,128]{1,0:T(8,128)S(1)} %constant_dynamic-slice_fusion.9), channel_id=1, source_target_pairs={{0,1},{1,0},{2,3},{3,2},{4,5},{5,4},{6,7},{7,6},{8,9},{9,8},{10,11... | collective-permute-start | bytes 2752520 | tf_op jit(solution)/shard_map/ppermute | solution.py:28
  31.1 2.2 %collective-permute-done = f32[1792,128]{1,0:T(8,128)} collective-permute-done((f32[1792,128]{1,0:T(8,128)S(1)}, f32[1792,128]{1,0:T(8,128)}, u32[]{:S(2)}, u32[]{:S(2)}) %collective-permute-start) | collective-permute-done | bytes 917536 | tf_op jit(solution)/shard_map/ppermute | solution.py:28
  36.6 11.7 %collective-permute-done.1 = f32[896,128]{1,0:T(8,128)S(1)} collective-permute-done((f32[896,128]{1,0:T(8,128)S(1)}, f32[896,128]{1,0:T(8,128)S(1)}, u32[]{:S(2)}, u32[]{:S(2)}) %collective-permute-start.1) | collective-permute-done | bytes 458784 | tf_op jit(solution)/shard_map/ppermute | solution.py:28
  48.3 1.9 collective-permute-start.2
  50.3 7.4 %collective-permute-done.2 = f32[448,128]{1,0:T(8,128)S(1)} collective-permute-done((f32[448,128]{1,0:T(8,128)S(1)}, f32[448,128]{1,0:T(8,128)S(1)}, u32[]{:S(2)}, u32[]{:S(2)}) %collective-permute-start.2) | collective-permute-done | bytes 229408 | tf_op jit(solution)/shard_map/ppermute | solution.py:28
  59.7 3.5 %collective-permute-done.3 = f32[224,128]{1,0:T(8,128)S(1)} collective-permute-done((f32[224,128]{1,0:T(8,128)S(1)}, f32[224,128]{1,0:T(8,128)S(1)}, u32[]{:S(2)}, u32[]{:S(2)}) %collective-permute-start.3) | collective-permute-done | bytes 114720 | tf_op jit(solution)/shard_map/ppermute | solution.py:28
  63.3 2.1 collective-permute-start.4
  65.4 3.0 %collective-permute-done.4 = f32[112,128]{1,0:T(8,128)S(1)} collective-permute-done((f32[112,128]{1,0:T(8,128)S(1)}, f32[112,128]{1,0:T(8,128)S(1)}, u32[]{:S(2)}, u32[]{:S(2)}) %collective-permute-start.4) | collective-permute-done | bytes 57376 | tf_op jit(solution)/shard_map/ppermute | solution.py:28
  68.4 1.9 collective-permute-start.5
  70.4 4.1 %collective-permute-done.5 = f32[56,128]{1,0:T(8,128)S(1)} collective-permute-done((f32[56,128]{1,0:T(8,128)S(1)}, f32[56,128]{1,0:T(8,128)S(1)}, u32[]{:S(2)}, u32[]{:S(2)}) %collective-permute-start.5) | collective-permute-done | bytes 28704 | tf_op jit(solution)/shard_map/ppermute | solution.py:28
  76.5 3.4 %collective-permute-done.6 = f32[28,128]{1,0:T(8,128)S(1)} collective-permute-done((f32[28,128]{1,0:T(8,128)S(1)}, f32[28,128]{1,0:T(8,128)S(1)}, u32[]{:S(2)}, u32[]{:S(2)}) %collective-permute-start.6) | collective-permute-done | bytes 14368 | tf_op jit(solution)/shard_map/ppermute | solution.py:28
  79.9 4.3 %collective-permute-start.7 = (f32[14,128]{1,0:T(8,128)S(1)}, f32[14,128]{1,0:T(8,128)S(1)}, u32[]{:S(2)}, u32[]{:S(2)}) collective-permute-start(f32[14,128]{1,0:T(8,128)S(1)} %constant_dynamic-slice_fusion.2), channel_id=1, source_target_pairs={{0,128},{1,129},{2,130},{3,131},{4,132},{5,133},{6,134},{7,135},{8... | collective-permute-start | bytes 21512 | tf_op jit(solution)/shard_map/ppermute | solution.py:28
  84.2 4.0 %collective-permute-done.7 = f32[14,128]{1,0:T(8,128)S(1)} collective-permute-done((f32[14,128]{1,0:T(8,128)S(1)}, f32[14,128]{1,0:T(8,128)S(1)}, u32[]{:S(2)}, u32[]{:S(2)}) %collective-permute-start.7) | collective-permute-done | bytes 7200 | tf_op jit(solution)/shard_map/ppermute | solution.py:28
  88.3 10.1 %collective-permute-start.8 = (f32[7,128]{1,0:T(8,128)S(1)}, f32[7,128]{1,0:T(8,128)S(1)}, u32[]{:S(2)}, u32[]{:S(2)}) collective-permute-start(f32[7,128]{1,0:T(8,128)S(1)} %constant_dynamic-slice_fusion), channel_id=1, source_target_pairs={{0,256},{1,257},{2,258},{3,259},{4,260},{5,261},{6,262},{7,263},{8... | collective-permute-start | bytes 10760 | tf_op jit(solution)/shard_map/ppermute | solution.py:28
  98.3 3.0 %collective-permute-done.8 = f32[7,128]{1,0:T(8,128)S(1)} collective-permute-done((f32[7,128]{1,0:T(8,128)S(1)}, f32[7,128]{1,0:T(8,128)S(1)}, u32[]{:S(2)}, u32[]{:S(2)}) %collective-permute-start.8) | collective-permute-done | bytes 3616 | tf_op jit(solution)/shard_map/ppermute | solution.py:28
  101.3 10.1 %collective-permute-start.9 = (f32[7,128]{1,0:T(8,128)S(1)}, f32[7,128]{1,0:T(8,128)S(1)}, u32[]{:S(2)}, u32[]{:S(2)}) collective-permute-start(f32[7,128]{1,0:T(8,128)S(1)} %fusion.5), channel_id=1, source_target_pairs={{0,256},{1,257},{2,258},{3,259},{4,260},{5,261},{6,262},{7,263},{8... | collective-permute-start | bytes 10760 | tf_op jit(solution)/shard_map/ppermute | solution.py:28
  111.4 3.0 %collective-permute-done.9 = f32[7,128]{1,0:T(8,128)S(1)} collective-permute-done((f32[7,128]{1,0:T(8,128)S(1)}, f32[7,128]{1,0:T(8,128)S(1)}, u32[]{:S(2)}, u32[]{:S(2)}) %collective-permute-start.9) | collective-permute-done | bytes 3616 | tf_op jit(solution)/shard_map/ppermute | solution.py:28
  114.4 4.3 %collective-permute-start.10 = (f32[14,128]{1,0:T(8,128)S(1)}, f32[14,128]{1,0:T(8,128)S(1)}, u32[]{:S(2)}, u32[]{:S(2)}) collective-permute-start(f32[14,128]{1,0:T(8,128)S(1)} %pad_maximum_fusion.5), channel_id=1, source_target_pairs={{0,128},{1,129},{2,130},{3,131},{4,132},{5,133},{6,134},{7,135},{8... | collective-permute-start | bytes 21512 | tf_op jit(solution)/shard_map/ppermute | solution.py:28
  118.7 4.3 %collective-permute-done.10 = f32[14,128]{1,0:T(8,128)S(1)} collective-permute-done((f32[14,128]{1,0:T(8,128)S(1)}, f32[14,128]{1,0:T(8,128)S(1)}, u32[]{:S(2)}, u32[]{:S(2)}) %collective-permute-start.10) | collective-permute-done | bytes 7200 | tf_op jit(solution)/shard_map/ppermute | solution.py:28
  123.0 1.9 collective-permute-start.11
  125.0 3.4 %collective-permute-done.11 = f32[28,128]{1,0:T(8,128)S(1)} collective-permute-done((f32[28,128]{1,0:T(8,128)S(1)}, f32[28,128]{1,0:T(8,128)S(1)}, u32[]{:S(2)}, u32[]{:S(2)}) %collective-permute-start.11) | collective-permute-done | bytes 14368 | tf_op jit(solution)/shard_map/ppermute | solution.py:28
  128.4 2.6 %collective-permute-start.12 = (f32[56,128]{1,0:T(8,128)S(1)}, f32[56,128]{1,0:T(8,128)S(1)}, u32[]{:S(2)}, u32[]{:S(2)}) collective-permute-start(f32[56,128]{1,0:T(8,128)S(1)} %pad_maximum_fusion.3), channel_id=1, source_target_pairs={{0,16},{1,17},{2,18},{3,19},{4,20},{5,21},{6,22},{7,23},{8,24},{9,... | collective-permute-start | bytes 86024 | tf_op jit(solution)/shard_map/ppermute | solution.py:28
  131.1 3.5 %collective-permute-done.12 = f32[56,128]{1,0:T(8,128)S(1)} collective-permute-done((f32[56,128]{1,0:T(8,128)S(1)}, f32[56,128]{1,0:T(8,128)S(1)}, u32[]{:S(2)}, u32[]{:S(2)}) %collective-permute-start.12) | collective-permute-done | bytes 28704 | tf_op jit(solution)/shard_map/ppermute | solution.py:28
  134.6 2.0 collective-permute-start.13
  136.6 3.2 %collective-permute-done.13 = f32[112,128]{1,0:T(8,128)S(1)} collective-permute-done((f32[112,128]{1,0:T(8,128)S(1)}, f32[112,128]{1,0:T(8,128)S(1)}, u32[]{:S(2)}, u32[]{:S(2)}) %collective-permute-start.13) | collective-permute-done | bytes 57376 | tf_op jit(solution)/shard_map/ppermute | solution.py:28
  139.8 1.9 collective-permute-start.14
  143.7 2.0 collective-permute-done.14
  149.8 5.2 %stack.80 = f32[8]{0:T(128)S(1)} concatenate(f32[1]{0:T(128)} %bitcast, f32[1]{0:T(128)} %bitcast.1, f32[1]{0:T(128)} %bitcast.2, f32[1]{0:T(128)} %bitcast.3, f32[1]{0:T(128)} %bitcast.20, f32[1]{0:T(128)} %bitcast.21, f32[1]{0:T(128)} %bitcast.23, f32[1]{0:T(128)} %bitcast.24), dimensions={0} | concatenate | bytes 64 | tf_op jit(solution)/shard_map/stack | solution.py:118
  155.2 26.8 %all-reduce = f32[64]{0:T(128)S(1)} all-reduce(f32[64]{0:T(128)S(1)} %dynamic-update-slice), channel_id=2, replica_groups=mesh['replica'=64,'shard'=8] {'shard'}, use_global_device_ids=true, to_apply=%add | all-reduce | flops 64 | bytes 512
  186.0 15.2 %all-gather.2 = bf16[8,1,49280]{2,1,0:T(2,128)(2,1)S(1)} all-gather(bf16[1,1,49280]{2,1,0:T(2,128)(2,1)S(1)} %reshape.157), channel_id=3, replica_groups=mesh['replica'=64,'shard'=8] {'shard'}, dimensions={0}, use_global_device_ids=true | all-gather | bytes 887040 | tf_op jit(solution)/shard_map/all_gather | solution.py:130
  (156 shorter events, 31.6 us)
Async XLA Ops:
  22.3 11.0 %collective-permute-start = (f32[1792,128]{1,0:T(8,128)S(1)}, f32[1792,128]{1,0:T(8,128)}, u32[]{:S(2)}, u32[]{:S(2)}) collective-permute-start(f32[1792,128]{1,0:T(8,128)S(1)} %constant_dynamic-slice_fusion.9), channel_id=1, source_target_pairs={{0,1},{1,0},{2,3},{3,2},{4,5},{5,4},{6,7},{7,6},{8,9},{9,8},{10,11... | collective-permute-start | bytes 2752520 | tf_op jit(solution)/shard_map/ppermute | solution.py:28
  34.6 13.6 %collective-permute-start.1 = (f32[896,128]{1,0:T(8,128)S(1)}, f32[896,128]{1,0:T(8,128)S(1)}, u32[]{:S(2)}, u32[]{:S(2)}) collective-permute-start(f32[896,128]{1,0:T(8,128)S(1)} %constant_dynamic-slice_fusion.8), channel_id=1, source_target_pairs={{0,2},{1,3},{2,0},{3,1},{4,6},{5,7},{6,4},{7,5},{8,10},{9,11},{10,... | collective-permute-start | bytes 1376264 | tf_op jit(solution)/shard_map/ppermute | solution.py:28
  48.3 9.3 %collective-permute-start.2 = (f32[448,128]{1,0:T(8,128)S(1)}, f32[448,128]{1,0:T(8,128)S(1)}, u32[]{:S(2)}, u32[]{:S(2)}) collective-permute-start(f32[448,128]{1,0:T(8,128)S(1)} %constant_dynamic-slice_fusion.7), channel_id=1, source_target_pairs={{0,4},{1,5},{2,6},{3,7},{4,0},{5,1},{6,2},{7,3},{8,12},{9,13},{10,... | collective-permute-start | bytes 688136 | tf_op jit(solution)/shard_map/ppermute | solution.py:28
  57.7 5.5 %collective-permute-start.3 = (f32[224,128]{1,0:T(8,128)S(1)}, f32[224,128]{1,0:T(8,128)S(1)}, u32[]{:S(2)}, u32[]{:S(2)}) collective-permute-start(f32[224,128]{1,0:T(8,128)S(1)} %constant_dynamic-slice_fusion.6), channel_id=1, source_target_pairs={{0,8},{1,9},{2,10},{3,11},{4,12},{5,13},{6,14},{7,15},{8,0},{9,1},... | collective-permute-start | bytes 344072 | tf_op jit(solution)/shard_map/ppermute | solution.py:28
  59.6 86.3 %copy-start.18 = (f32[64]{0:T(128)S(1)}, f32[64]{0:T(128)}, u32[]{:S(2)}) copy-start(f32[64]{0:T(128)} %param.22) | copy-start | bytes 772
  59.6 86.3 %copy-start.19 = (f32[64]{0:T(128)S(1)}, f32[64]{0:T(128)}, u32[]{:S(2)}) copy-start(f32[64]{0:T(128)} %param.30) | copy-start | bytes 772
  59.6 86.3 %copy-start.20 = (f32[64]{0:T(128)S(1)}, f32[64]{0:T(128)}, u32[]{:S(2)}) copy-start(f32[64]{0:T(128)} %param.26) | copy-start | bytes 772
  59.7 87.5 %copy-start.15 = (f32[4,6]{1,0:T(4,128)S(1)}, f32[4,6]{1,0:T(4,128)}, u32[]{:S(2)}) copy-start(f32[4,6]{1,0:T(4,128)} %param.23) | copy-start | bytes 292
  59.7 87.4 %copy-start.16 = (f32[4,6]{1,0:T(4,128)S(1)}, f32[4,6]{1,0:T(4,128)}, u32[]{:S(2)}) copy-start(f32[4,6]{1,0:T(4,128)} %param.31) | copy-start | bytes 292
  59.7 87.4 %copy-start.17 = (f32[4,6]{1,0:T(4,128)S(1)}, f32[4,6]{1,0:T(4,128)}, u32[]{:S(2)}) copy-start(f32[4,6]{1,0:T(4,128)} %param.27) | copy-start | bytes 292
  63.2 85.2 %copy-start.3 = (f32[64,384]{1,0:T(8,128)S(1)}, f32[64,384]{1,0:T(8,128)}, u32[]{:S(2)}) copy-start(f32[64,384]{1,0:T(8,128)} %param.20) | copy-start | bytes 294916
  63.2 85.1 %copy-start.9 = (f32[64,384]{1,0:T(8,128)S(1)}, f32[64,384]{1,0:T(8,128)}, u32[]{:S(2)}) copy-start(f32[64,384]{1,0:T(8,128)} %param.28) | copy-start | bytes 294916
  63.3 85.1 %copy-start.10 = (f32[64,384]{1,0:T(8,128)S(1)}, f32[64,384]{1,0:T(8,128)}, u32[]{:S(2)}) copy-start(f32[64,384]{1,0:T(8,128)} %param.24) | copy-start | bytes 294916
  63.3 5.1 %collective-permute-start.4 = (f32[112,128]{1,0:T(8,128)S(1)}, f32[112,128]{1,0:T(8,128)S(1)}, u32[]{:S(2)}, u32[]{:S(2)}) collective-permute-start(f32[112,128]{1,0:T(8,128)S(1)} %constant_dynamic-slice_fusion.5), channel_id=1, source_target_pairs={{0,32},{1,33},{2,34},{3,35},{4,36},{5,37},{6,38},{7,39},{8,40},{9,... | collective-permute-start | bytes 172040 | tf_op jit(solution)/shard_map/ppermute | solution.py:28
  68.4 6.1 %collective-permute-start.5 = (f32[56,128]{1,0:T(8,128)S(1)}, f32[56,128]{1,0:T(8,128)S(1)}, u32[]{:S(2)}, u32[]{:S(2)}) collective-permute-start(f32[56,128]{1,0:T(8,128)S(1)} %constant_dynamic-slice_fusion.4), channel_id=1, source_target_pairs={{0,16},{1,17},{2,18},{3,19},{4,20},{5,21},{6,22},{7,23},{8,24},{9,... | collective-permute-start | bytes 86024 | tf_op jit(solution)/shard_map/ppermute | solution.py:28
  70.3 78.8 %copy-start.2 = (f32[48,512]{1,0:T(8,128)S(1)}, f32[48,512]{1,0:T(8,128)}, u32[]{:S(2)}) copy-start(f32[48,512]{1,0:T(8,128)} %param.21) | copy-start | bytes 294916
  70.3 78.8 %copy-start.11 = (f32[48,512]{1,0:T(8,128)S(1)}, f32[48,512]{1,0:T(8,128)}, u32[]{:S(2)}) copy-start(f32[48,512]{1,0:T(8,128)} %param.29) | copy-start | bytes 294916
  70.3 78.7 %copy-start.12 = (f32[48,512]{1,0:T(8,128)S(1)}, f32[48,512]{1,0:T(8,128)}, u32[]{:S(2)}) copy-start(f32[48,512]{1,0:T(8,128)} %param.25) | copy-start | bytes 294916
  74.5 5.4 %collective-permute-start.6 = (f32[28,128]{1,0:T(8,128)S(1)}, f32[28,128]{1,0:T(8,128)S(1)}, u32[]{:S(2)}, u32[]{:S(2)}) collective-permute-start(f32[28,128]{1,0:T(8,128)S(1)} %constant_dynamic-slice_fusion.3), channel_id=1, source_target_pairs={{0,64},{1,65},{2,66},{3,67},{4,68},{5,69},{6,70},{7,71},{8,72},{9,... | collective-permute-start | bytes 43016 | tf_op jit(solution)/shard_map/ppermute | solution.py:28
  79.9 8.3 %collective-permute-start.7 = (f32[14,128]{1,0:T(8,128)S(1)}, f32[14,128]{1,0:T(8,128)S(1)}, u32[]{:S(2)}, u32[]{:S(2)}) collective-permute-start(f32[14,128]{1,0:T(8,128)S(1)} %constant_dynamic-slice_fusion.2), channel_id=1, source_target_pairs={{0,128},{1,129},{2,130},{3,131},{4,132},{5,133},{6,134},{7,135},{8... | collective-permute-start | bytes 21512 | tf_op jit(solution)/shard_map/ppermute | solution.py:28
  88.3 13.1 %collective-permute-start.8 = (f32[7,128]{1,0:T(8,128)S(1)}, f32[7,128]{1,0:T(8,128)S(1)}, u32[]{:S(2)}, u32[]{:S(2)}) collective-permute-start(f32[7,128]{1,0:T(8,128)S(1)} %constant_dynamic-slice_fusion), channel_id=1, source_target_pairs={{0,256},{1,257},{2,258},{3,259},{4,260},{5,261},{6,262},{7,263},{8... | collective-permute-start | bytes 10760 | tf_op jit(solution)/shard_map/ppermute | solution.py:28
  101.3 13.1 %collective-permute-start.9 = (f32[7,128]{1,0:T(8,128)S(1)}, f32[7,128]{1,0:T(8,128)S(1)}, u32[]{:S(2)}, u32[]{:S(2)}) collective-permute-start(f32[7,128]{1,0:T(8,128)S(1)} %fusion.5), channel_id=1, source_target_pairs={{0,256},{1,257},{2,258},{3,259},{4,260},{5,261},{6,262},{7,263},{8... | collective-permute-start | bytes 10760 | tf_op jit(solution)/shard_map/ppermute | solution.py:28
  114.4 8.6 %collective-permute-start.10 = (f32[14,128]{1,0:T(8,128)S(1)}, f32[14,128]{1,0:T(8,128)S(1)}, u32[]{:S(2)}, u32[]{:S(2)}) collective-permute-start(f32[14,128]{1,0:T(8,128)S(1)} %pad_maximum_fusion.5), channel_id=1, source_target_pairs={{0,128},{1,129},{2,130},{3,131},{4,132},{5,133},{6,134},{7,135},{8... | collective-permute-start | bytes 21512 | tf_op jit(solution)/shard_map/ppermute | solution.py:28
  123.0 5.4 %collective-permute-start.11 = (f32[28,128]{1,0:T(8,128)S(1)}, f32[28,128]{1,0:T(8,128)S(1)}, u32[]{:S(2)}, u32[]{:S(2)}) collective-permute-start(f32[28,128]{1,0:T(8,128)S(1)} %pad_maximum_fusion.4), channel_id=1, source_target_pairs={{0,64},{1,65},{2,66},{3,67},{4,68},{5,69},{6,70},{7,71},{8,72},{9,... | collective-permute-start | bytes 43016 | tf_op jit(solution)/shard_map/ppermute | solution.py:28
  128.4 6.1 %collective-permute-start.12 = (f32[56,128]{1,0:T(8,128)S(1)}, f32[56,128]{1,0:T(8,128)S(1)}, u32[]{:S(2)}, u32[]{:S(2)}) collective-permute-start(f32[56,128]{1,0:T(8,128)S(1)} %pad_maximum_fusion.3), channel_id=1, source_target_pairs={{0,16},{1,17},{2,18},{3,19},{4,20},{5,21},{6,22},{7,23},{8,24},{9,... | collective-permute-start | bytes 86024 | tf_op jit(solution)/shard_map/ppermute | solution.py:28
  134.6 5.2 %collective-permute-start.13 = (f32[112,128]{1,0:T(8,128)S(1)}, f32[112,128]{1,0:T(8,128)S(1)}, u32[]{:S(2)}, u32[]{:S(2)}) collective-permute-start(f32[112,128]{1,0:T(8,128)S(1)} %pad_maximum_fusion.2), channel_id=1, source_target_pairs={{0,32},{1,33},{2,34},{3,35},{4,36},{5,37},{6,38},{7,39},{8,40},{9,... | collective-permute-start | bytes 172040 | tf_op jit(solution)/shard_map/ppermute | solution.py:28
  139.8 5.8 %collective-permute-start.14 = (f32[224,128]{1,0:T(8,128)S(1)}, f32[224,128]{1,0:T(8,128)S(1)}, u32[]{:S(2)}, u32[]{:S(2)}) collective-permute-start(f32[224,128]{1,0:T(8,128)S(1)} %pad_maximum_fusion.1), channel_id=1, source_target_pairs={{0,8},{1,9},{2,10},{3,11},{4,12},{5,13},{6,14},{7,15},{8,0},{9,1},... | collective-permute-start | bytes 344072 | tf_op jit(solution)/shard_map/ppermute | solution.py:28
  149.1 52.2 %copy-start.4 = (f32[64,384]{1,0:T(8,128)}, f32[64,384]{1,0:T(8,128)S(1)}, u32[]{:S(2)}) copy-start(f32[64,384]{1,0:T(8,128)S(1)} %get-tuple-element.70) | copy-start | bytes 294916
  149.1 52.1 %copy-start.5 = (f32[64,384]{1,0:T(8,128)}, f32[64,384]{1,0:T(8,128)S(1)}, u32[]{:S(2)}) copy-start(f32[64,384]{1,0:T(8,128)S(1)} %get-tuple-element.71) | copy-start | bytes 294916
  149.8 51.5 %copy-start.6 = (f32[48,512]{1,0:T(8,128)}, f32[48,512]{1,0:T(8,128)S(1)}, u32[]{:S(2)}) copy-start(f32[48,512]{1,0:T(8,128)S(1)} %get-tuple-element.68) | copy-start | bytes 294916
  149.8 51.6 %copy-start.7 = (f32[48,512]{1,0:T(8,128)}, f32[48,512]{1,0:T(8,128)S(1)}, u32[]{:S(2)}) copy-start(f32[48,512]{1,0:T(8,128)S(1)} %get-tuple-element.69) | copy-start | bytes 294916
  182.2 19.1 %copy-start.13 = (f32[4]{0:T(128)}, f32[4]{0:T(128)S(1)}, u32[]{:S(2)}) copy-start(f32[4]{0:T(128)S(1)} %get-tuple-element.123) | copy-start | bytes 52
  (4 other events, 17.2 us)
